TPU v7x, 128 devices: a whole 4x4x4 slice. The times are simulated.
128 devices in a mesh: group: 16 (over x, z), mp: 8 (over y, core).
Axes of the slice: x: 4, y: 4, z: 4, core: 2. Of those that a mesh axis runs over, the one named last changes fastest.
Arguments:
- stream: bfloat16 [8192, 3584], P('group', 'mp'), may hold values from -6 to 6
- prenorm_gain: float32 [3584], replicated, may hold values from 0.25 to 12
- query_weight: bfloat16 [3584, 4096], P(None, 'mp'), may hold values from -0.09375 to 0.09375
- key_weight: bfloat16 [3584, 2048], P(None, 'mp'), may hold values from -0.09375 to 0.09375
- value_weight: bfloat16 [3584, 2048], P(None, 'mp'), may hold values from -0.09375 to 0.09375
- output_weight: bfloat16 [4096, 3584], P('mp'), may hold values from -0.09375 to 0.09375
- adapter_down_rows: bfloat16 [64, 16, 3584], P('group', None, 'mp'), may hold values from -0.09375 to 0.09375
- adapter_up_query: bfloat16 [64, 16, 4096], P('group', None, 'mp'), may hold values from -1.5 to 1.5
- request_adapter: int32 [16, 4], replicated, may hold values from 0 to 63
- adapter_row_index: int32 [64], replicated, may hold values from 0 to 63, each once
- request_token_length: int32 [16, 4], replicated, may hold values from 1 to 256, 512 in all within a row
- continues_previous: int32 [16], replicated, may hold values from 0 to 1, as said below
- request_cache_block: int32 [16, 4], replicated, may hold values from 0 to 31, as said below
- cached_length: int32 [16, 4], replicated, may hold values from 1 to 256
- cached_rotated_keys: bfloat16 [32, 256, 2048], P('group', None, 'mp'), may hold values from -6 to 6
- cached_value_rows: bfloat16 [32, 256, 2048], P('group', None, 'mp'), may hold values from -6 to 6
Outputs:
- attn_out: bfloat16 [8192, 3584], P('group', 'mp')
Inputs may be any that keep to these rules, and one draw needn't show every extreme that they name: `continues_previous`: the first group has 0; some group has 1. `request_cache_block`: the owner of block b is group b // 2; blocks may be shared by requests.
All inputs are finite; a program needn't handle non-finite values.
Results may differ from a plain program's by a relative error of at most 0.017.
The roundings to bfloat16 on the way count: a program that leaves them out, or rounds other values in their place, can miss the bound.
Values may be sent and summed in bfloat16 or wider, within the bound.
No kernel may reach another device: no remote copies, remote signals or barrier semaphores. Data moves between devices by JAX's collectives and lax.ppermute only.
A program may use at most 128 MiB of HBM per device.

v0:
```python
import jax
import jax.numpy as jnp
from jax import lax
from jax.sharding import PartitionSpec as P

HEAD_WIDTH = 256
REQS = 4
adapter_scale = 2.0


def shifted(value, axis, steps):
    count = lax.axis_size(axis)
    first, last = (max(0, -steps), min(count, count - steps))
    return lax.ppermute(value, axis, [(source, source + steps) for source in range(first, last)])


def rotate(values, position, head_size):
    count = values.shape[0]
    shaped = values.reshape(count, -1, head_size)
    half = head_size // 2
    freq = 10000.0 ** (-jnp.arange(half, dtype=jnp.float32) / half)
    angle = position[:, None, None] * freq[None, None, :]
    cosine = jnp.cos(angle)
    sine = jnp.sin(angle)
    first = shaped[..., :half]
    second = shaped[..., half:]
    turned = jnp.concatenate(
        [first * cosine - second * sine, second * cosine + first * sine], axis=-1
    )
    return turned.reshape(count, -1)


def layout(lengths, cached, split_flag, prev_len, count):
    ends = jnp.cumsum(lengths)
    starts = ends - lengths
    place = jnp.arange(count, dtype=jnp.int32)
    member = ((place[:, None] >= starts[None, :]) & (place[:, None] < ends[None, :])).astype(
        jnp.int32
    )
    request = jnp.sum(member * jnp.arange(lengths.shape[0], dtype=jnp.int32)[None, :], axis=1)
    offset = place - jnp.sum(member * starts[None, :], axis=1)
    extra = jnp.where(request == 0, split_flag * prev_len, 0)
    position = jnp.sum(member * cached[None, :], axis=1) + extra + offset
    return (member, request, position.astype(jnp.float32))


def attend(
    query_vectors,
    keys,
    values,
    prev_keys,
    prev_values,
    cache_keys,
    cache_values,
    request,
    cached,
    split_flag,
    prev_len,
    head_size,
):
    count = query_vectors.shape[0]
    kv_heads = keys.shape[1] // head_size
    ratio = query_vectors.shape[1] // keys.shape[1]
    block = cache_keys.shape[1]
    slots = cache_keys.shape[0] * block
    every_key = jnp.concatenate([cache_keys.reshape(slots, -1), prev_keys, keys], 0).reshape(
        -1, kv_heads, head_size
    )
    every_value = jnp.concatenate(
        [cache_values.reshape(slots, -1), prev_values, values], 0
    ).reshape(-1, kv_heads, head_size)
    slot_req = jnp.arange(slots, dtype=jnp.int32) // block
    slot_col = jnp.arange(slots, dtype=jnp.int32) % block
    cache_ok = (request[:, None] == slot_req[None, :]) & (
        slot_col[None, :] < cached[slot_req][None, :]
    )
    place = jnp.arange(count, dtype=jnp.int32)
    prev_ok = (split_flag == 1) & (request[:, None] == 0) & (place[None, :] >= count - prev_len)
    own_ok = (request[:, None] == request[None, :]) & (place[None, :] <= place[:, None])
    allowed = jnp.concatenate([cache_ok, prev_ok, own_ok], 1)
    grouped = query_vectors.reshape(count, kv_heads, ratio, head_size)
    scores = jnp.einsum(
        "tkrd,skd->krts", grouped, every_key, preferred_element_type=jnp.float32
    ) * head_size ** (-0.5)
    scores = jnp.where(allowed[None, None], scores, jnp.float32(-1e30))
    top = jnp.max(scores, axis=-1, keepdims=True)
    weights = jnp.exp(scores - top)
    total = jnp.sum(weights, axis=-1)
    numer = jnp.einsum(
        "krts,skd->tkrd",
        weights.astype(jnp.bfloat16),
        every_value,
        preferred_element_type=jnp.float32,
    )
    result = numer / jnp.transpose(total, (2, 0, 1))[..., None]
    return result.reshape(count, -1).astype(jnp.bfloat16)


def on_device(
    stream,
    prenorm_gain,
    query_weight,
    key_weight,
    value_weight,
    output_weight,
    adapter_down_rows,
    adapter_up_query,
    request_adapter,
    adapter_row_index,
    request_token_length,
    continues_previous,
    request_cache_block,
    cached_length,
    cached_rotated_keys,
    cached_value_rows,
):
    count = stream.shape[0]
    width = stream.shape[1]
    group_at = lax.axis_index("group")
    model_at = lax.axis_index("mp")
    whole = lax.all_gather(stream, "mp", axis=1, tiled=True)
    wide = whole.astype(jnp.float32)
    normalized_input = (
        wide * lax.rsqrt(jnp.mean(wide * wide, axis=1, keepdims=True) + 1e-06) * prenorm_gain
    ).astype(jnp.bfloat16)
    normed_part = lax.dynamic_slice_in_dim(normalized_input, model_at * width, width, 1)
    before = jnp.maximum(group_at - 1, 0)
    lengths = request_token_length[group_at]
    cached = cached_length[group_at]
    split_flag = continues_previous[group_at]
    prev_len = request_token_length[before, REQS - 1]
    member, request, position = layout(lengths, cached, split_flag, prev_len, count)
    wanted = adapter_row_index[request_adapter[group_at]]
    pieces = (
        lax.all_gather(adapter_down_rows, "group", axis=0, tiled=True),
        lax.all_gather(adapter_up_query, "group", axis=0, tiled=True),
    )
    stored = jnp.arange(pieces[0].shape[0], dtype=jnp.int32)
    onehot = (wanted[:, None] == stored[None, :]).astype(jnp.bfloat16)
    new_down = jnp.einsum("rj,jkd->rkd", onehot, pieces[0], preferred_element_type=jnp.float32)
    new_up = jnp.einsum("rj,jkd->rkd", onehot, pieces[1], preferred_element_type=jnp.float32)
    chosen_down = new_down.astype(jnp.bfloat16)
    chosen_up = new_up.astype(jnp.bfloat16)
    rank_index = adapter_down_rows.shape[1]
    partial_low = jnp.einsum(
        "td,rkd->trk", normed_part, chosen_down, preferred_element_type=jnp.float32
    ).reshape(count, REQS * rank_index)
    low = lax.psum(partial_low, "mp").astype(jnp.bfloat16)
    own_columns = jnp.repeat(member, rank_index, axis=1).astype(jnp.bfloat16)
    query_update = jnp.dot(
        low * own_columns,
        chosen_up.reshape(REQS * rank_index, -1),
        preferred_element_type=jnp.float32,
    )
    query_vectors = (
        jnp.dot(normalized_input, query_weight, preferred_element_type=jnp.float32)
        + adapter_scale * query_update
    )
    query_vectors = rotate(query_vectors, position, HEAD_WIDTH).astype(jnp.bfloat16)
    keys = rotate(
        jnp.dot(normalized_input, key_weight, preferred_element_type=jnp.float32),
        position,
        HEAD_WIDTH,
    ).astype(jnp.bfloat16)
    values = jnp.dot(normalized_input, value_weight, preferred_element_type=jnp.float32).astype(
        jnp.bfloat16
    )
    prev_keys, prev_values = shifted((keys, values), "group", 1)
    blocks = request_cache_block[group_at]
    pieces = (
        lax.all_gather(cached_rotated_keys, "group", axis=0, tiled=True),
        lax.all_gather(cached_value_rows, "group", axis=0, tiled=True),
    )
    stored = jnp.arange(pieces[0].shape[0], dtype=jnp.int32)
    onehot = (blocks[:, None] == stored[None, :]).astype(jnp.bfloat16)
    new_keys = jnp.einsum("rj,jcd->rcd", onehot, pieces[0], preferred_element_type=jnp.float32)
    new_values = jnp.einsum("rj,jcd->rcd", onehot, pieces[1], preferred_element_type=jnp.float32)
    cache_keys = new_keys.astype(jnp.bfloat16)
    cache_values = new_values.astype(jnp.bfloat16)
    attended = attend(
        query_vectors,
        keys,
        values,
        prev_keys,
        prev_values,
        cache_keys,
        cache_values,
        request,
        cached,
        split_flag,
        prev_len,
        HEAD_WIDTH,
    )
    partial_out = jnp.dot(attended, output_weight, preferred_element_type=jnp.float32)
    return lax.psum_scatter(partial_out.astype(jnp.bfloat16), "mp", scatter_dimension=1, tiled=True)


def solution(mesh):
    placed = (
        P("group", "mp"),
        P(),
        P(None, "mp"),
        P(None, "mp"),
        P(None, "mp"),
        P("mp", None),
        P("group", None, "mp"),
        P("group", None, "mp"),
        P(),
        P(),
        P(),
        P(),
        P(),
        P(),
        P("group", None, "mp"),
        P("group", None, "mp"),
    )
    return jax.shard_map(
        on_device, mesh=mesh, in_specs=placed, out_specs=P("group", "mp"), check_vma=False
    )
```

profile of v0, /device:TPU:0, one launch (start us, length us, event | category | flops | bytes accessed | tf_op | source)
XLA Modules:
  0.0 254.0 jit_solution(16617972660007501374)
XLA Ops:
  6.5 0.7 all-gather.11.cloned.1.call-update
  7.3 0.7 all-gather.7.cloned.1.call-update
  8.1 0.7 all-gather.5.cloned.1.call-update
  8.8 0.5 all-gather.9.cloned.1.call-update
  9.4 1.3 constant_dynamic-slice_fusion.2
  10.7 0.9 dynamic-slice_reduce_fusion
  11.9 0.9 fusion.79
  12.8 0.6 fusion.81
  13.4 26.9 %all_gather.18 = bf16[64,16,448]{2,1,0:T(8,128)(2,1)S(1)} all-gather(bf16[4,16,448]{2,1,0:T(8,128)(2,1)} %param.22), channel_id=1, replica_groups=mesh['group'=16,'mp'=8] {'group'}, dimensions={0}, use_global_device_ids=true | all-gather | bytes 974848 | tf_op jit(solution)/shard_map/all_gather | solution.py:135
  40.9 2.6 %compare_select_fusion.1 = s32[1024,1]{0,1:T(1,128)S(1)} fusion(s32[]{:T(128)} %bitcast.7, s32[]{:T(128)} %bitcast.8, s32[]{:T(128)} %bitcast.10, s32[]{:T(128)} %bitcast.9), kind=kLoop, calls=%fused_computation.71 | loop fusion | flops 17408 | bytes 4112 | tf_op jit(solution)/shard_map/gather | solution.py:75
  43.5 1.2 dynamic_slice.24
  46.8 0.9 dynamic-slice_reduce_fusion.1
  47.6 1.3 gather_fusion
  49.5 1.8 multiply_cosine_fusion
  51.4 0.8 compare_and_fusion
  52.2 1.2 convolution_convert_fusion.3
  53.8 1.2 all-gather.11.cloned.1.call-done
  54.9 2.4 convolution_convert_fusion.2
  57.4 28.5 %all-gather.7.cloned.1.call-done = bf16[512,3584]{0,1:T(8,128)(2,1)} async-done(((bf16[512,448]{0,1:T(8,128)(2,1)}), bf16[512,3584]{0,1:T(8,128)(2,1)}) %all-gather.7.cloned.1.call-update) | async-done | bytes 3670032 | tf_op jit(solution)/shard_map/all_gather | solution.py:121
  85.8 3.0 %fusion.2 = f32[512]{0:T(512)S(1)} fusion(bf16[512,3584]{0,1:T(8,128)(2,1)} %all-gather.7.cloned.1.call-done), kind=kLoop, calls=%fused_computation.7 | loop fusion | flops 5504512 | bytes 3672064 | tf_op jit(solution)/shard_map/reduce_sum | solution.py:124
  89.0 1.6 fusion.4
  90.6 1.8 copy-done.2
  92.4 1.9 convolution_convert_fusion.1
  94.3 1.8 copy.47
  96.1 4.2 %collective-permute-start = (bf16[512,256]{1,0:T(8,128)(2,1)}, bf16[512,256]{1,0:T(8,128)(2,1)}, u32[]{:S(2)}, u32[]{:S(2)}) collective-permute-start(bf16[512,256]{1,0:T(8,128)(2,1)} %convolution_convert_fusion.1), channel_id=1, source_target_pairs={{0,8},{8,16},{16,24},{24,32},{32,40},{40,48},{48,56},{56,64},{64,7... | collective-permute-start | bytes 786440 | tf_op jit(solution)/shard_map/ppermute | solution.py:14
  100.2 3.8 %convolution_bitcast_fusion = f32[512,1,256]{0,2,1:T(8,128)S(1)} fusion(bf16[512,3584]{0,1:T(8,128)(2,1)} %copy-done.2, bf16[3584,256]{1,0:T(8,128)(2,1)} %param.19), kind=kOutput, calls=%fused_computation.26 | convolution fusion | flops 939524096 | bytes 6029312 | tf_op jit(solution)/shard_map/dot_general | solution.py:161
  104.0 1.2 fusion.49
  105.2 0.7 maximum_bitcast_fusion.6
  105.9 1.8 copy.52
  107.7 3.4 %collective-permute-start.1 = (bf16[512,256]{0,1:T(8,128)(2,1)}, bf16[512,256]{0,1:T(8,128)(2,1)}, u32[]{:S(2)}, u32[]{:S(2)}) collective-permute-start(bf16[512,256]{0,1:T(8,128)(2,1)} %maximum_bitcast_fusion.6), channel_id=1, source_target_pairs={{0,8},{8,16},{16,24},{24,32},{32,40},{40,48},{48,56},{56,64},{64,7... | collective-permute-start | bytes 786440 | tf_op jit(solution)/shard_map/ppermute | solution.py:14
  111.1 1.2 fusion.41
  112.3 26.0 %all-reduce.1 = bf16[512,64]{0,1:T(8,128)(2,1)S(1)} all-reduce(f32[512,64]{0,1:T(8,128)S(1)} %bitcast.101), channel_id=1, replica_groups=mesh['group'=16,'mp'=8] {'mp'}, use_global_device_ids=true, to_apply=%region_5.6 | all-reduce | flops 32768 | bytes 196608 | tf_op jit(solution)/shard_map/psum | solution.py:148
  138.4 5.3 %fusion.82 = f32[512,512]{0,1:T(8,128)S(1)} fusion(bf16[512,3584]{0,1:T(8,128)(2,1)} %copy-done.2, bf16[3584,512]{1,0:T(8,128)(2,1)} %param.18), kind=kOutput, calls=%fused_computation.129 | convolution fusion | flops 1879048192 | bytes 8388608 | tf_op jit(solution)/shard_map/dot_general | solution.py:156
  144.0 1.1 fusion.80
  145.1 1.2 copy.63
  146.4 2.1 copy.62
  148.5 2.2 subtract_convert_fusion
  150.6 1.8 copy.46
  152.5 1.8 copy.51
  154.3 4.6 %fusion.18 = bf16[4,256,256]{2,0,1:T(4,128)(2,1)S(1)} fusion(bf16[32,256,256]{2,1,0:T(8,128)(2,1)} %all-gather.5.cloned.1.call-done, s32[4]{0:T(128)S(1)} %dynamic-slice_reduce_fusion.1), kind=kOutput, calls=%fused_computation.24 | convolution fusion | flops 17039488 | bytes 4718608 | tf_op jit(solution)/shard_map/rj,jcd->rcd/dot_general | solution.py:177
  159.0 1.0 copy.45
  160.0 35.3 %all-gather.9.cloned.1.call-done = bf16[32,256,256]{2,1,0:T(8,128)(2,1)} async-done(((bf16[2,256,256]{2,1,0:T(8,128)(2,1)}), bf16[32,256,256]{2,1,0:T(8,128)(2,1)}) %all-gather.9.cloned.1.call-update) | async-done | bytes 4194320 | tf_op jit(solution)/shard_map/all_gather | solution.py:171
  195.3 4.7 %fusion.21 = bf16[4,256,256]{2,0,1:T(4,128)(2,1)S(1)} fusion(bf16[32,256,256]{2,1,0:T(8,128)(2,1)} %all-gather.9.cloned.1.call-done, s32[4]{0:T(128)S(1)} %dynamic-slice_reduce_fusion.1), kind=kOutput, calls=%fused_computation.25 | convolution fusion | flops 17039488 | bytes 4718608 | tf_op jit(solution)/shard_map/rj,jcd->rcd/dot_general | solution.py:176
  200.1 1.8 fusion.5
  201.9 2.2 fusion
  204.2 2.8 %divide_convert_fusion = bf16[512,1,2,256]{0,3,2,1:T(8,128)(2,1)S(1)} fusion(f32[2048,512,2]{1,0,2:T(8,128)S(1)} %get-tuple-element.25, f32[2,512]{1,0:T(2,128)S(1)} %get-tuple-element.24, pred[512,2048]{0,1:T(8,128)(4,1)S(1)} %pad_add_fusion, bf16[512,256]{0,1:T(8,128)(2,1)S(1)} %copy-done.4, bf16[512,256]{0,1:T(8,128)(2,1)S(1)} %copy-done.6, ...), kind=kOutput, calls=%fused_computation.43 | convolution fusion | flops 1085800448 | bytes 11018240 | tf_op jit(solution)/shard_map/krts,skd->tkrd/dot_general | solution.py:89
  207.0 3.9 %convolution_convert_fusion = bf16[512,3584]{0,1:T(8,128)(2,1)} fusion(bf16[512,512]{0,1:T(8,128)(2,1)S(1)} %bitcast.107, bf16[512,3584]{1,0:T(8,128)(2,1)S(1)} %copy-done.11), kind=kOutput, calls=%fused_computation.11 | convolution fusion | flops 1880883200 | bytes 7864320 | tf_op jit(solution)/shard_map/dot_general | solution.py:194
  210.9 36.5 %reduce-scatter.2.cloned.1.call-done = bf16[512,448]{0,1:T(8,128)(2,1)} async-done(((bf16[512,3584]{0,1:T(8,128)(2,1)}), bf16[512,448]{0,1:T(8,128)(2,1)}) %reduce-scatter.2.cloned.1.call-update) | async-done | bytes 458768 | tf_op jit(solution)/shard_map/reduce_scatter | solution.py:195
  (54 shorter events, 2.1 us)
Async XLA Ops:
  6.5 85.8 %copy-start = (bf16[3584,256]{1,0:T(8,128)(2,1)S(1)}, bf16[3584,256]{1,0:T(8,128)(2,1)}, u32[]{:S(2)}) copy-start(bf16[3584,256]{1,0:T(8,128)(2,1)} %param.20) | copy-start | bytes 5505028
  6.5 48.4 %all-gather.11.cloned.1.call-start = ((), (), s32[]{:S(2)}) async-start(), calls=%async_computation.4 | async-start | bytes 1114112 | tf_op jit(solution)/shard_map/all_gather | solution.py:136
  7.3 78.6 %all-gather.7.cloned.1.call-start = ((), (), s32[]{:S(2)}) async-start(), calls=%async_computation.2 | async-start | bytes 4128768 | tf_op jit(solution)/shard_map/all_gather | solution.py:121
  8.0 146.3 %all-gather.5.cloned.1.call-start = ((), (), s32[]{:S(2)}) async-start(), calls=%async_computation.1 | async-start | bytes 4456448 | tf_op jit(solution)/shard_map/all_gather | solution.py:172
  8.7 186.5 %all-gather.9.cloned.1.call-start = ((), (), s32[]{:S(2)}) async-start(), calls=%async_computation.3 | async-start | bytes 4456448 | tf_op jit(solution)/shard_map/all_gather | solution.py:171
  9.3 238.1 %reduce-scatter.2.cloned.1.call-start = ((), (), s32[]{:S(2)}) async-start(), calls=%async_computation.5 | async-start | bytes 4128768 | tf_op jit(solution)/shard_map/reduce_scatter | solution.py:195
  53.4 35.5 %copy-start.10 = (f32[3584]{0:T(1024)S(1)}, f32[3584]{0:T(1024)}, u32[]{:S(2)}) copy-start(f32[3584]{0:T(1024)} %param.17) | copy-start | bytes 43012
  85.8 3.1 %copy-start.1 = (bf16[512,3584]{0,1:T(8,128)(2,1)S(1)}, bf16[512,3584]{0,1:T(8,128)(2,1)}, u32[]{:S(2)}) copy-start(bf16[512,3584]{0,1:T(8,128)(2,1)} %all-gather.7.cloned.1.call-done) | copy-start | bytes 11010052
  90.5 1.8 copy-start.2
  96.1 54.6 %collective-permute-start = (bf16[512,256]{1,0:T(8,128)(2,1)}, bf16[512,256]{1,0:T(8,128)(2,1)}, u32[]{:S(2)}, u32[]{:S(2)}) collective-permute-start(bf16[512,256]{1,0:T(8,128)(2,1)} %convolution_convert_fusion.1), channel_id=1, source_target_pairs={{0,8},{8,16},{16,24},{24,32},{32,40},{40,48},{48,56},{56,64},{64,7... | collective-permute-start | bytes 786440 | tf_op jit(solution)/shard_map/ppermute | solution.py:14
  107.7 44.8 %collective-permute-start.1 = (bf16[512,256]{0,1:T(8,128)(2,1)}, bf16[512,256]{0,1:T(8,128)(2,1)}, u32[]{:S(2)}, u32[]{:S(2)}) collective-permute-start(bf16[512,256]{0,1:T(8,128)(2,1)} %maximum_bitcast_fusion.6), channel_id=1, source_target_pairs={{0,8},{8,16},{16,24},{24,32},{32,40},{40,48},{48,56},{56,64},{64,7... | collective-permute-start | bytes 786440 | tf_op jit(solution)/shard_map/ppermute | solution.py:14
  160.0 40.1 %copy-start.5 = (bf16[512,256]{1,0:T(8,128)(2,1)S(1)}, bf16[512,256]{1,0:T(8,128)(2,1)}, u32[]{:S(2)}) copy-start(bf16[512,256]{1,0:T(8,128)(2,1)} %copy.52) | copy-start | bytes 786436
  160.0 40.1 %copy-start.7 = (bf16[512,256]{1,0:T(8,128)(2,1)S(1)}, bf16[512,256]{1,0:T(8,128)(2,1)}, u32[]{:S(2)}) copy-start(bf16[512,256]{1,0:T(8,128)(2,1)} %copy.51) | copy-start | bytes 786436
  195.3 4.8 %copy-start.8 = (bf16[512,2,128]{2,0,1:T(8,128)(2,1)S(1)}, bf16[512,2,128]{2,0,1:T(8,128)(2,1)}, u32[]{:S(2)}) copy-start(bf16[512,2,128]{2,0,1:T(8,128)(2,1)} %get-tuple-element.12) | copy-start | bytes 786436
  195.3 4.8 %copy-start.9 = (bf16[512,2,128]{2,0,1:T(8,128)(2,1)S(1)}, bf16[512,2,128]{2,0,1:T(8,128)(2,1)}, u32[]{:S(2)}) copy-start(bf16[512,2,128]{2,0,1:T(8,128)(2,1)} %get-tuple-element.13) | copy-start | bytes 786436
  201.9 2.2 copy-start.3
  201.9 2.2 copy-start.4
  201.9 2.2 copy-start.6
  204.2 2.8 %copy-start.11 = (bf16[512,3584]{1,0:T(8,128)(2,1)S(1)}, bf16[512,3584]{1,0:T(8,128)(2,1)}, u32[]{:S(2)}) copy-start(bf16[512,3584]{1,0:T(8,128)(2,1)} %param.21) | copy-start | bytes 11010052
Sparse Core Ops, SparseCore 0:
  9.5 45.3 all-gather.10
  56.6 29.1 all-gather.6
  88.0 53.9 all-gather.4
  144.0 51.2 all-gather.8
  211.0 36.3 reduce-scatter.1
where the time goes:
time: 255 us; the launch traced here: 254 us
  waiting for transfers between devices  104 us (41%)
  blocking collectives  52.9 us (21%)
  matrix products  33.9 us (13%)
  local copies, waits for them, and re-layouts  21.9 us (9%)
  other arithmetic  17.3 us (7%)
  between operations  16.1 us (6%)
  starting transfers between devices  7.77 us (3%)
    reduce_scatter x1, waiting for transfers between devices, on_device(): lax.psum_scatter(partial_out.astype(jnp.bfloat16), 'mp', scatter_dimensio...  36.5 us
    all_gather x1, waiting for transfers between devices, on_device(): lax.all_gather(cached_rotated_keys, 'group', axis=0, tiled=True)  35.3 us
    all_gather x1, waiting for transfers between devices, on_device(): whole = lax.all_gather(stream, 'mp', axis=1, tiled=True)  28.5 us
    all_gather x1, blocking collectives, on_device(): lax.all_gather(adapter_down_rows, 'group', axis=0, tiled=True)  26.9 us
    psum x1, blocking collectives, on_device(): low = lax.psum(partial_low, 'mp').astype(jnp.bfloat16)  26 us
    ppermute x2, starting transfers between devices, shifted(): lax.ppermute(value, axis, [(source, source + steps) for source in range(f...  7.62 us
    unnamed x27, local copies, waits for them, and re-layouts  5.37 us
    dot_general x1, matrix products, on_device(): jnp.dot(normalized_input, query_weight, preferred_element_type=jnp.float32)  5.26 us
  transfers between devices with their start and end apart: 7, of which 4 were waited for; matrix products, arithmetic and copies ran while one was open for 22% of the time, Pallas kernels for 0%

commit v1 on v0

--- a/solution.py
+++ b/solution.py
@@ -6,6 +6,12 @@
 HEAD_WIDTH = 256
 REQS = 4
 adapter_scale = 2.0
+
+
+def joined_along(blocks, dim):
+    blocks = jnp.moveaxis(blocks, 0, dim)
+    lengths = blocks.shape
+    return blocks.reshape(*lengths[:dim], lengths[dim] * lengths[dim + 1], *lengths[dim + 2 :])
 
 
 def shifted(value, axis, steps):
@@ -118,7 +124,19 @@
     width = stream.shape[1]
     group_at = lax.axis_index("group")
     model_at = lax.axis_index("mp")
-    whole = lax.all_gather(stream, "mp", axis=1, tiled=True)
+    devices = lax.axis_size("mp")
+    pairs = [(i, (i + 1) % devices) for i in range(devices)]
+    back = [(b, a) for a, b in pairs]
+    lower, upper = ([], [])
+    for step in range(devices - 1):
+        if step % 2 == 0:
+            lower.append(lax.ppermute(lower[-1] if lower else stream, "mp", pairs))
+        else:
+            upper.append(lax.ppermute(upper[-1] if upper else stream, "mp", back))
+    tiles = jnp.stack([*lower[::-1], stream, *upper])
+    shift = lax.axis_index("mp") - len(lower)
+    tiles = tiles[(jnp.arange(devices) - shift) % devices]
+    whole = joined_along(tiles, 1)
     wide = whole.astype(jnp.float32)
     normalized_input = (
         wide * lax.rsqrt(jnp.mean(wide * wide, axis=1, keepdims=True) + 1e-06) * prenorm_gain

time: 255 us -> 231 us (0.906)
  waiting for transfers between devices: 104 us -> 54.1 us
  local copies, waits for them, and re-layouts: 21.9 us -> 37.7 us
  starting transfers between devices: 7.77 us -> 15 us
    all_gather x1, waiting for transfers between devices: 35.3 us -> 0.01 us  [on_device(): lax.all_gather(cached_rotated_keys, 'group', axis=0, tiled=True)]
    all_gather x1 -> x0, waiting for transfers between devices: 28.5 us -> none  [on_device(): whole = lax.all_gather(stream, 'mp', axis=1, tiled=True)]
    ppermute x0 -> x7, waiting for transfers between devices: none -> 18.5 us  [the longest x4 18.5 us: on_device(): lower.append(lax.ppermute(lower[-1] if lower else stream, 'mp', pairs))]
    unnamed x27 -> x36, local copies, waits for them, and re-layouts: 5.37 us -> 16.3 us
    ppermute x0 -> x7, starting transfers between devices: none -> 8.9 us  [the longest x3 8.87 us: on_device(): upper.append(lax.ppermute(upper[-1] if upper else stream, 'mp', back))]
    gather x0 -> x1, local copies, waits for them, and re-layouts: none -> 4.75 us  [on_device(): tiles = tiles[(jnp.arange(devices) - shift) % devices]]
  transfers between devices with their start and end apart: 7 -> 13, of which waited for: 4 -> 4; matrix products, arithmetic and copies ran while one was open for 22% -> 32% of each run, Pallas kernels for 0% -> 0%
where the time goes in v1:
time: 231 us; the launch traced here: 230 us
  waiting for transfers between devices  54.1 us (23%)
  blocking collectives  52.9 us (23%)
  local copies, waits for them, and re-layouts  37.7 us (16%)
  matrix products  34.2 us (15%)
  other arithmetic  19.7 us (9%)
  between operations  15.9 us (7%)
  starting transfers between devices  15 us (6%)
    reduce_scatter x1, waiting for transfers between devices, on_device(): lax.psum_scatter(partial_out.astype(jnp.bfloat16), 'mp', scatter_dimensio...  34.2 us
    all_gather x1, blocking collectives, on_device(): lax.all_gather(adapter_down_rows, 'group', axis=0, tiled=True)  27.6 us
    psum x1, blocking collectives, on_device(): low = lax.psum(partial_low, 'mp').astype(jnp.bfloat16)  25.3 us
    ppermute x4, waiting for transfers between devices, on_device(): lower.append(lax.ppermute(lower[-1] if lower else stream, 'mp', pairs))  18.5 us
    unnamed x36, local copies, waits for them, and re-layouts  16.3 us
    ppermute x3, starting transfers between devices, on_device(): upper.append(lax.ppermute(upper[-1] if upper else stream, 'mp', back))  8.87 us
    ppermute x2, starting transfers between devices, shifted(): lax.ppermute(value, axis, [(source, source + steps) for source in range(f...  5.99 us
    dot_general x1, matrix products, on_device(): jnp.dot(normalized_input, query_weight, preferred_element_type=jnp.float32)  5.41 us
  transfers between devices with their start and end apart: 13, of which 4 were waited for; matrix products, arithmetic and copies ran while one was open for 32% of the time, Pallas kernels for 0%

profile of v1, /device:TPU:0, one launch (start us, length us, event | category | flops | bytes accessed | tf_op | source)
XLA Modules:
  0.0 229.6 jit_solution(16639754433139359199)
XLA Ops:
  8.1 2.9 %collective-permute-start.4 = (bf16[512,448]{0,1:T(8,128)(2,1)}, bf16[512,448]{0,1:T(8,128)(2,1)}, u32[]{:S(2)}, u32[]{:S(2)}) collective-permute-start(bf16[512,448]{0,1:T(8,128)(2,1)} %param.16), channel_id=1, source_target_pairs={{1,0},{2,1},{3,2},{4,3},{5,4},{6,5},{7,6},{0,7},{9,8},{10,9},{11,1... | collective-permute-start | bytes 1376264 | tf_op jit(solution)/shard_map/ppermute | solution.py:135
  11.1 1.3 constant_dynamic-slice_fusion.2
  13.0 1.2 dynamic_slice.24
  19.8 27.6 %all_gather.14 = bf16[64,16,448]{2,1,0:T(8,128)(2,1)S(1)} all-gather(bf16[4,16,448]{2,1,0:T(8,128)(2,1)} %param.22), channel_id=1, replica_groups=mesh['group'=16,'mp'=8] {'group'}, dimensions={0}, use_global_device_ids=true | all-gather | bytes 974848 | tf_op jit(solution)/shard_map/all_gather | solution.py:153
  47.3 1.3 gather_fusion.1
  49.5 2.5 %compare_select_fusion.1 = s32[1024,1]{0,1:T(1,128)S(1)} fusion(s32[]{:T(128)} %bitcast.18, s32[]{:T(128)} %bitcast.19, s32[]{:T(128)} %bitcast.21, s32[]{:T(128)} %bitcast.20), kind=kLoop, calls=%fused_computation.79 | loop fusion | flops 17408 | bytes 4112 | tf_op jit(solution)/shard_map/gather | solution.py:81
  52.1 1.8 multiply_cosine_fusion
  54.7 8.6 %collective-permute-done.1 = bf16[512,448]{0,1:T(8,128)(2,1)} collective-permute-done((bf16[512,448]{0,1:T(8,128)(2,1)}, bf16[512,448]{0,1:T(8,128)(2,1)}, u32[]{:S(2)}, u32[]{:S(2)}) %collective-permute-start.1) | collective-permute-done | bytes 458784 | tf_op jit(solution)/shard_map/ppermute | solution.py:133
  63.3 1.2 convolution_convert_fusion.3
  64.8 3.0 %collective-permute-start.5 = (bf16[512,448]{0,1:T(8,128)(2,1)}, bf16[512,448]{0,1:T(8,128)(2,1)S(1)}, u32[]{:S(2)}, u32[]{:S(2)}) collective-permute-start(bf16[512,448]{0,1:T(8,128)(2,1)} %collective-permute-done.4), channel_id=1, source_target_pairs={{1,0},{2,1},{3,2},{4,3},{5,4},{6,5},{7,6},{0,7},{9,8},{10,9},{11,1... | collective-permute-start | bytes 1376264 | tf_op jit(solution)/shard_map/ppermute | solution.py:135
  67.7 5.0 %collective-permute-done.2 = bf16[512,448]{0,1:T(8,128)(2,1)} collective-permute-done((bf16[512,448]{0,1:T(8,128)(2,1)}, bf16[512,448]{0,1:T(8,128)(2,1)}, u32[]{:S(2)}, u32[]{:S(2)}) %collective-permute-start.2) | collective-permute-done | bytes 458784 | tf_op jit(solution)/shard_map/ppermute | solution.py:133
  72.8 1.4 pad_add_fusion
  74.2 3.0 %collective-permute-start.6 = (bf16[512,448]{0,1:T(8,128)(2,1)S(1)}, bf16[512,448]{0,1:T(8,128)(2,1)S(1)}, u32[]{:S(2)}, u32[]{:S(2)}) collective-permute-start(bf16[512,448]{0,1:T(8,128)(2,1)S(1)} %collective-permute-done.5), channel_id=1, source_target_pairs={{1,0},{2,1},{3,2},{4,3},{5,4},{6,5},{7,6},{0,7},{9,8},{10,9},{11,1... | collective-permute-start | bytes 1376264 | tf_op jit(solution)/shard_map/ppermute | solution.py:135
  77.2 4.9 %collective-permute-done.3 = bf16[512,448]{0,1:T(8,128)(2,1)S(1)} collective-permute-done((bf16[512,448]{0,1:T(8,128)(2,1)}, bf16[512,448]{0,1:T(8,128)(2,1)S(1)}, u32[]{:S(2)}, u32[]{:S(2)}) %collective-permute-start.3) | collective-permute-done | bytes 458784 | tf_op jit(solution)/shard_map/ppermute | solution.py:133
  82.9 1.9 bitcast_dynamic-update-slice_fusion.6
  84.8 1.8 bitcast_dynamic-update-slice_fusion.5
  86.6 1.9 bitcast_dynamic-update-slice_fusion.4
  88.5 1.9 bitcast_dynamic-update-slice_fusion.3
  90.3 1.8 bitcast_dynamic-update-slice_fusion.2
  93.8 4.7 %gather_fusion = bf16[8,512,448]{1,2,0:T(8,128)(2,1)} fusion(bf16[8,512,448]{1,2,0:T(8,128)(2,1)} %bitcast_dynamic-update-slice_fusion, s32[1024]{0:T(1024)S(1)} %pad_clamp_fusion.1), kind=kCustom, calls=%fused_computation | custom fusion | bytes 7340064 | tf_op jit(solution)/shard_map/gather | solution.py:138
  98.5 3.1 %multiply_reduce_fusion = f32[512]{0:T(512)S(1)} fusion(bf16[8,512,448]{1,2,0:T(8,128)(2,1)} %gather_fusion), kind=kLoop, calls=%fused_computation.9 | loop fusion | flops 5504512 | bytes 3672064 | tf_op jit(solution)/shard_map/reduce_sum | solution.py:142
  101.8 1.6 fusion.3
  103.4 1.8 copy-done.2
  105.2 1.9 convolution_convert_fusion.1
  107.1 1.8 copy.47
  108.9 3.1 %collective-permute-start.7 = (bf16[512,256]{1,0:T(8,128)(2,1)}, bf16[512,256]{1,0:T(8,128)(2,1)}, u32[]{:S(2)}, u32[]{:S(2)}) collective-permute-start(bf16[512,256]{1,0:T(8,128)(2,1)} %convolution_convert_fusion.1), channel_id=1, source_target_pairs={{0,8},{8,16},{16,24},{24,32},{32,40},{40,48},{48,56},{56,64},{64,7... | collective-permute-start | bytes 786440 | tf_op jit(solution)/shard_map/ppermute | solution.py:20
  112.0 3.8 %convolution_bitcast_fusion = f32[512,1,256]{0,2,1:T(8,128)S(1)} fusion(bf16[512,3584]{0,1:T(8,128)(2,1)} %copy-done.2, bf16[3584,256]{1,0:T(8,128)(2,1)} %param.19), kind=kOutput, calls=%fused_computation.26 | convolution fusion | flops 939524096 | bytes 6029312 | tf_op jit(solution)/shard_map/dot_general | solution.py:179
  115.8 1.2 fusion.47
  117.7 1.8 copy.52
  119.5 2.9 %collective-permute-start.8 = (bf16[512,256]{0,1:T(8,128)(2,1)}, bf16[512,256]{0,1:T(8,128)(2,1)}, u32[]{:S(2)}, u32[]{:S(2)}) collective-permute-start(bf16[512,256]{0,1:T(8,128)(2,1)} %maximum_bitcast_fusion.6), channel_id=1, source_target_pairs={{0,8},{8,16},{16,24},{24,32},{32,40},{40,48},{48,56},{56,64},{64,7... | collective-permute-start | bytes 786440 | tf_op jit(solution)/shard_map/ppermute | solution.py:20
  122.3 1.2 fusion.39
  123.5 25.3 %all-reduce.1 = bf16[512,64]{0,1:T(8,128)(2,1)S(1)} all-reduce(f32[512,64]{0,1:T(8,128)S(1)} %bitcast.127), channel_id=1, replica_groups=mesh['group'=16,'mp'=8] {'mp'}, use_global_device_ids=true, to_apply=%region_5.6 | all-reduce | flops 32768 | bytes 196608 | tf_op jit(solution)/shard_map/psum | solution.py:166
  149.0 2.5 %convolution_convert_fusion.2 = bf16[4,16,512]{2,0,1:T(4,128)(2,1)S(1)} fusion(bf16[64,16,512]{2,1,0:T(8,128)(2,1)} %all-gather.8.cloned.1.call-done, s32[4]{0:T(128)S(1)} %gather_fusion.1), kind=kOutput, calls=%fused_computation.28 | convolution fusion | flops 4227328 | bytes 1114128 | tf_op jit(solution)/shard_map/rj,jkd->rkd/dot_general | solution.py:159
  151.8 5.4 %convolution_add_fusion = f32[512,512]{0,1:T(8,128)S(1)} fusion(f32[512,512]{0,1:T(8,128)S(1)} %convolution_multiply_fusion, bf16[512,3584]{0,1:T(8,128)(2,1)} %copy-done.2, bf16[3584,512]{1,0:T(8,128)(2,1)} %param.18), kind=kOutput, calls=%fused_computation.23 | convolution fusion | flops 1879310336 | bytes 9437184 | tf_op jit(solution)/shard_map/dot_general | solution.py:174
  157.2 1.1 fusion.80
  158.3 1.2 copy.63
  159.6 2.1 copy.62
  161.7 2.1 subtract_convert_fusion
  163.8 1.8 copy.46
  165.6 1.8 copy.51
  167.4 4.6 %fusion.16 = bf16[4,256,256]{2,0,1:T(4,128)(2,1)S(1)} fusion(bf16[32,256,256]{2,1,0:T(8,128)(2,1)} %all-gather.4.cloned.1.call-done, s32[4]{0:T(128)S(1)} %dynamic-slice_reduce_fusion.1), kind=kOutput, calls=%fused_computation.24 | convolution fusion | flops 17039488 | bytes 4718608 | tf_op jit(solution)/shard_map/rj,jcd->rcd/dot_general | solution.py:195
  172.1 1.0 copy.45
  173.2 4.7 %fusion.19 = bf16[4,256,256]{2,0,1:T(4,128)(2,1)S(1)} fusion(bf16[32,256,256]{2,1,0:T(8,128)(2,1)} %all-gather.6.cloned.1.call-done, s32[4]{0:T(128)S(1)} %dynamic-slice_reduce_fusion.1), kind=kOutput, calls=%fused_computation.25 | convolution fusion | flops 17039488 | bytes 4718608 | tf_op jit(solution)/shard_map/rj,jcd->rcd/dot_general | solution.py:194
  178.0 1.9 fusion.4
  179.9 2.2 fusion
  182.1 2.8 %divide_convert_fusion = bf16[512,1,2,256]{0,3,2,1:T(8,128)(2,1)S(1)} fusion(f32[2048,512,2]{1,0,2:T(8,128)S(1)} %get-tuple-element.25, f32[2,512]{1,0:T(2,128)S(1)} %get-tuple-element.24, pred[512,2048]{0,1:T(8,128)(4,1)S(1)} %pad_add_fusion, bf16[512,256]{0,1:T(8,128)(2,1)S(1)} %copy-done.4, bf16[512,256]{0,1:T(8,128)(2,1)S(1)} %copy-done.6, ...), kind=kOutput, calls=%fused_computation.43 | convolution fusion | flops 1085800448 | bytes 11018240 | tf_op jit(solution)/shard_map/krts,skd->tkrd/dot_general | solution.py:95
  185.0 3.9 %convolution_convert_fusion = bf16[512,3584]{0,1:T(8,128)(2,1)} fusion(bf16[512,512]{0,1:T(8,128)(2,1)S(1)} %bitcast.133, bf16[512,3584]{1,0:T(8,128)(2,1)S(1)} %copy-done.12), kind=kOutput, calls=%fused_computation.11 | convolution fusion | flops 1880883200 | bytes 7864320 | tf_op jit(solution)/shard_map/dot_general | solution.py:212
  188.9 34.2 %reduce-scatter.2.cloned.1.call-done = bf16[512,448]{0,1:T(8,128)(2,1)} async-done(((bf16[512,3584]{0,1:T(8,128)(2,1)}), bf16[512,448]{0,1:T(8,128)(2,1)}) %reduce-scatter.2.cloned.1.call-update) | async-done | bytes 458768 | tf_op jit(solution)/shard_map/reduce_scatter | solution.py:213
  (78 shorter events, 11.3 us)
Async XLA Ops:
  6.5 98.7 %copy-start = (bf16[3584,256]{1,0:T(8,128)(2,1)S(1)}, bf16[3584,256]{1,0:T(8,128)(2,1)}, u32[]{:S(2)}) copy-start(bf16[3584,256]{1,0:T(8,128)(2,1)} %param.20) | copy-start | bytes 5505028
  6.5 58.0 %copy-start.11 = (s32[16,4]{0,1:T(4,128)S(1)}, s32[16,4]{0,1:T(4,128)}, u32[]{:S(2)}) copy-start(s32[16,4]{0,1:T(4,128)} %param.28) | copy-start | bytes 772
  6.5 142.4 %all-gather.8.cloned.1.call-start = ((), (), s32[]{:S(2)}) async-start(), calls=%async_computation.3 | async-start | bytes 1114112 | tf_op jit(solution)/shard_map/all_gather | solution.py:154
  7.3 160.2 %all-gather.4.cloned.1.call-start = ((), (), s32[]{:S(2)}) async-start(), calls=%async_computation.1 | async-start | bytes 4456448 | tf_op jit(solution)/shard_map/all_gather | solution.py:190
  8.0 165.1 %all-gather.6.cloned.1.call-start = ((), (), s32[]{:S(2)}) async-start(), calls=%async_computation.2 | async-start | bytes 4456448 | tf_op jit(solution)/shard_map/all_gather | solution.py:189
  8.1 45.8 %collective-permute-start = (bf16[512,448]{0,1:T(8,128)(2,1)}, bf16[512,448]{0,1:T(8,128)(2,1)}, u32[]{:S(2)}, u32[]{:S(2)}) collective-permute-start(bf16[512,448]{0,1:T(8,128)(2,1)} %param.16), channel_id=1, source_target_pairs={{0,1},{1,2},{2,3},{3,4},{4,5},{5,6},{6,7},{7,0},{8,9},{9,10},{10,1... | collective-permute-start | bytes 1376264 | tf_op jit(solution)/shard_map/ppermute | solution.py:133
  8.1 56.7 %collective-permute-start.4 = (bf16[512,448]{0,1:T(8,128)(2,1)}, bf16[512,448]{0,1:T(8,128)(2,1)}, u32[]{:S(2)}, u32[]{:S(2)}) collective-permute-start(bf16[512,448]{0,1:T(8,128)(2,1)} %param.16), channel_id=1, source_target_pairs={{1,0},{2,1},{3,2},{4,3},{5,4},{6,5},{7,6},{0,7},{9,8},{10,9},{11,1... | collective-permute-start | bytes 1376264 | tf_op jit(solution)/shard_map/ppermute | solution.py:135
  11.0 212.0 %reduce-scatter.2.cloned.1.call-start = ((), (), s32[]{:S(2)}) async-start(), calls=%async_computation.4 | async-start | bytes 4128768 | tf_op jit(solution)/shard_map/reduce_scatter | solution.py:213
  53.9 9.4 %collective-permute-start.1 = (bf16[512,448]{0,1:T(8,128)(2,1)}, bf16[512,448]{0,1:T(8,128)(2,1)}, u32[]{:S(2)}, u32[]{:S(2)}) collective-permute-start(bf16[512,448]{0,1:T(8,128)(2,1)} %collective-permute-done), channel_id=1, source_target_pairs={{0,1},{1,2},{2,3},{3,4},{4,5},{5,6},{6,7},{7,0},{8,9},{9,10},{10,1... | collective-permute-start | bytes 1376264 | tf_op jit(solution)/shard_map/ppermute | solution.py:133
  63.3 9.4 %collective-permute-start.2 = (bf16[512,448]{0,1:T(8,128)(2,1)}, bf16[512,448]{0,1:T(8,128)(2,1)}, u32[]{:S(2)}, u32[]{:S(2)}) collective-permute-start(bf16[512,448]{0,1:T(8,128)(2,1)} %collective-permute-done.1), channel_id=1, source_target_pairs={{0,1},{1,2},{2,3},{3,4},{4,5},{5,6},{6,7},{7,0},{8,9},{9,10},{10,1... | collective-permute-start | bytes 1376264 | tf_op jit(solution)/shard_map/ppermute | solution.py:133
  64.8 9.5 %collective-permute-start.5 = (bf16[512,448]{0,1:T(8,128)(2,1)}, bf16[512,448]{0,1:T(8,128)(2,1)S(1)}, u32[]{:S(2)}, u32[]{:S(2)}) collective-permute-start(bf16[512,448]{0,1:T(8,128)(2,1)} %collective-permute-done.4), channel_id=1, source_target_pairs={{1,0},{2,1},{3,2},{4,3},{5,4},{6,5},{7,6},{0,7},{9,8},{10,9},{11,1... | collective-permute-start | bytes 1376264 | tf_op jit(solution)/shard_map/ppermute | solution.py:135
  72.7 9.3 %collective-permute-start.3 = (bf16[512,448]{0,1:T(8,128)(2,1)}, bf16[512,448]{0,1:T(8,128)(2,1)S(1)}, u32[]{:S(2)}, u32[]{:S(2)}) collective-permute-start(bf16[512,448]{0,1:T(8,128)(2,1)} %collective-permute-done.2), channel_id=1, source_target_pairs={{0,1},{1,2},{2,3},{3,4},{4,5},{5,6},{6,7},{7,0},{8,9},{9,10},{10,1... | collective-permute-start | bytes 1376264 | tf_op jit(solution)/shard_map/ppermute | solution.py:133
  74.2 18.7 %collective-permute-start.6 = (bf16[512,448]{0,1:T(8,128)(2,1)S(1)}, bf16[512,448]{0,1:T(8,128)(2,1)S(1)}, u32[]{:S(2)}, u32[]{:S(2)}) collective-permute-start(bf16[512,448]{0,1:T(8,128)(2,1)S(1)} %collective-permute-done.5), channel_id=1, source_target_pairs={{1,0},{2,1},{3,2},{4,3},{5,4},{6,5},{7,6},{0,7},{9,8},{10,9},{11,1... | collective-permute-start | bytes 1376264 | tf_op jit(solution)/shard_map/ppermute | solution.py:135
  93.8 7.9 %copy-start.10 = (f32[3584]{0:T(1024)S(1)}, f32[3584]{0:T(1024)}, u32[]{:S(2)}) copy-start(f32[3584]{0:T(1024)} %param.17) | copy-start | bytes 43012
  98.5 3.3 %copy-start.1 = (bf16[8,512,448]{1,2,0:T(8,128)(2,1)S(1)}, bf16[8,512,448]{1,2,0:T(8,128)(2,1)}, u32[]{:S(2)}) copy-start(bf16[8,512,448]{1,2,0:T(8,128)(2,1)} %gather_fusion) | copy-start | bytes 11010052
  103.4 1.8 copy-start.2
  108.9 54.9 %collective-permute-start.7 = (bf16[512,256]{1,0:T(8,128)(2,1)}, bf16[512,256]{1,0:T(8,128)(2,1)}, u32[]{:S(2)}, u32[]{:S(2)}) collective-permute-start(bf16[512,256]{1,0:T(8,128)(2,1)} %convolution_convert_fusion.1), channel_id=1, source_target_pairs={{0,8},{8,16},{16,24},{24,32},{32,40},{40,48},{48,56},{56,64},{64,7... | collective-permute-start | bytes 786440 | tf_op jit(solution)/shard_map/ppermute | solution.py:20
  119.5 46.1 %collective-permute-start.8 = (bf16[512,256]{0,1:T(8,128)(2,1)}, bf16[512,256]{0,1:T(8,128)(2,1)}, u32[]{:S(2)}, u32[]{:S(2)}) collective-permute-start(bf16[512,256]{0,1:T(8,128)(2,1)} %maximum_bitcast_fusion.6), channel_id=1, source_target_pairs={{0,8},{8,16},{16,24},{24,32},{32,40},{40,48},{48,56},{56,64},{64,7... | collective-permute-start | bytes 786440 | tf_op jit(solution)/shard_map/ppermute | solution.py:20
  173.1 4.8 %copy-start.5 = (bf16[512,256]{1,0:T(8,128)(2,1)S(1)}, bf16[512,256]{1,0:T(8,128)(2,1)}, u32[]{:S(2)}) copy-start(bf16[512,256]{1,0:T(8,128)(2,1)} %copy.52) | copy-start | bytes 786436
  173.1 4.8 %copy-start.7 = (bf16[512,256]{1,0:T(8,128)(2,1)S(1)}, bf16[512,256]{1,0:T(8,128)(2,1)}, u32[]{:S(2)}) copy-start(bf16[512,256]{1,0:T(8,128)(2,1)} %copy.51) | copy-start | bytes 786436
  173.1 4.8 %copy-start.8 = (bf16[512,2,128]{2,0,1:T(8,128)(2,1)S(1)}, bf16[512,2,128]{2,0,1:T(8,128)(2,1)}, u32[]{:S(2)}) copy-start(bf16[512,2,128]{2,0,1:T(8,128)(2,1)} %get-tuple-element.12) | copy-start | bytes 786436
  173.2 4.8 %copy-start.9 = (bf16[512,2,128]{2,0,1:T(8,128)(2,1)S(1)}, bf16[512,2,128]{2,0,1:T(8,128)(2,1)}, u32[]{:S(2)}) copy-start(bf16[512,2,128]{2,0,1:T(8,128)(2,1)} %get-tuple-element.13) | copy-start | bytes 786436
  179.9 2.2 copy-start.3
  179.9 2.2 copy-start.4
  179.9 2.2 copy-start.6
  182.1 2.8 %copy-start.12 = (bf16[512,3584]{1,0:T(8,128)(2,1)S(1)}, bf16[512,3584]{1,0:T(8,128)(2,1)}, u32[]{:S(2)}) copy-start(bf16[512,3584]{1,0:T(8,128)(2,1)} %param.21) | copy-start | bytes 11010052
Sparse Core Ops, SparseCore 0:
  9.5 45.5 all-gather.7
  57.2 50.7 all-gather.3
  110.2 52.4 all-gather.5
  189.0 33.9 reduce-scatter.1
